TPU v7x, 128 devices: a whole 4x4x4 slice. The times are simulated.
128 devices in a mesh: seq: 64 (over z, x, y_lo, core), chan: 2 (over y_hi).
Axes of the slice: x: 4, y: 4 (y_hi: 2, y_lo: 2; y = y_hi * 2 + y_lo), z: 4, core: 2. Of those that a mesh axis runs over, the one named last changes fastest.
Arguments:
- signal: bfloat16 [2, 32768, 128], P('chan', 'seq'), may hold values from -6 to 6
- cotangent: bfloat16 [2, 32768, 128], P('chan', 'seq'), may hold values from -6 to 6
- band_freq: int32 [16], replicated, may hold values from 1 to 8191
- w_embed: float32 [32, 64], replicated, may hold values from -2 to 2
- b_embed: float32 [64], replicated, may hold values from -3.140625 to 3.140625
- w_out: float32 [64, 128], P(None, 'chan'), may hold values from -0.75 to 0.75
- decay: float32 [128], P('chan'), may hold values from 0.25 to 16, as said below
Outputs:
- conv_out: bfloat16 [2, 32768, 128], P('chan', 'seq')
- d_signal: bfloat16 [2, 32768, 128], P('chan', 'seq')
- grad_embed: float32 [32, 64], replicated
- grad_bias: float32 [64], replicated
- grad_out: float32 [64, 128], P(None, 'chan')
Inputs may be any that keep to these rules, and one draw needn't show every extreme that they name: decay rates are positive.
All inputs are finite; a program needn't handle non-finite values.
Results may differ from a plain program's by a relative error of at most 0.007.
Values may be sent and summed in bfloat16 or wider, within the bound.
No kernel may reach another device: no remote copies, remote signals or barrier semaphores. Data moves between devices by JAX's collectives and lax.ppermute only.
A program may use at most 192 MiB of HBM per device.

v0:
```python
import math
import jax
import jax.numpy as jnp
from jax import lax
from jax.sharding import PartitionSpec as P

exact_mode = lax.Precision.HIGHEST


def mat_dot(lhs_mat, rhs_mat):
    return jnp.dot(lhs_mat, rhs_mat, preferred_element_type=jnp.float32, precision=exact_mode)


def band_phase(band_freq, places, seq_total):
    upper_part = places // 1024
    lower_part = places % 1024
    partial_turn = upper_part[:, None] * band_freq[None, :] % seq_total
    wrapped = (partial_turn * 1024 + lower_part[:, None] * band_freq[None, :]) % seq_total
    return wrapped.astype(jnp.float32) * (2.0 * math.pi / seq_total)


def filter_parts(places, band_freq, w_embed, b_embed, w_out, decay, seq_total):
    phases = band_phase(band_freq, places, seq_total)
    features = jnp.concatenate([jnp.cos(phases), jnp.sin(phases)], axis=1)
    preact = mat_dot(features, w_embed) + b_embed[None, :]
    hidden = jnp.sin(preact)
    fraction = places.astype(jnp.float32) / seq_total
    envelope = (
        jnp.exp(-decay[None, :] * fraction[:, None]) * jnp.sqrt((1.0 + decay) / seq_total)[None, :]
    )
    taps = mat_dot(hidden, w_out) * envelope
    return (features, preact, hidden, taps, envelope)


def angle_table(rows_idx, cols_idx, modulus):
    wrapped = rows_idx[:, None] * cols_idx[None, :] % modulus
    angles = wrapped.astype(jnp.float32) * (2.0 * math.pi / modulus)
    return (jnp.cos(angles), jnp.sin(angles))


def local(signal, cotangent, band_freq, w_embed, b_embed, w_out, decay):
    devices = lax.axis_size("seq")
    rank_seq = lax.axis_index("seq")
    seg_len = signal.shape[1] * 2
    channels = signal.shape[2] // 2
    block_w = seg_len // devices
    width = block_w * channels
    rows_all = 2 * devices
    pair = rows_all // devices
    seq_total = seg_len * devices
    fft_size = 2 * seq_total
    inv_scale = 1.0 / fft_size
    n_arr = 3
    dev_ids = jnp.arange(devices, dtype=jnp.int32)
    row_ids = jnp.arange(rows_all, dtype=jnp.int32)
    blk_ids = jnp.arange(block_w, dtype=jnp.int32)
    lane_blk = jnp.arange(width, dtype=jnp.int32) // channels
    b_lane = rank_seq * block_w + lane_blk
    src = jnp.stack([signal.reshape(devices, width), cotangent.reshape(devices, width)], axis=1)
    cols = lax.all_to_all(src, "seq", split_axis=0, concat_axis=0, tiled=True)
    places = (dev_ids[:, None] * seg_len + rank_seq * block_w + blk_ids[None, :]).reshape(-1)
    features, preact, hidden, taps, envelope = filter_parts(
        places, band_freq, w_embed, b_embed, w_out, decay, seq_total
    )
    stacked = jnp.concatenate(
        [cols.astype(jnp.float32), taps.reshape(devices, 1, width)], axis=1
    ).reshape(devices, n_arr * width)
    col_cos, col_sin = angle_table(row_ids, dev_ids, rows_all)
    y_re = mat_dot(col_cos, stacked).reshape(rows_all, n_arr, width)
    y_im = -mat_dot(col_sin, stacked).reshape(rows_all, n_arr, width)
    tw_cos, tw_sin = angle_table(row_ids, b_lane, fft_size)
    tw_cos = tw_cos[:, None, :]
    tw_sin = tw_sin[:, None, :]
    t_re = y_re * tw_cos + y_im * tw_sin
    t_im = y_im * tw_cos - y_re * tw_sin
    spec = jnp.stack([t_re, t_im], axis=1)
    spec = lax.all_to_all(spec, "seq", split_axis=0, concat_axis=0, tiled=True)
    q_cos, q_sin = angle_table(dev_ids, dev_ids, devices)
    stage_a = mat_dot(jnp.concatenate([q_cos, q_sin], axis=0), spec.reshape(devices, -1))
    stage_a = stage_a.reshape(2, devices, pair, 2, n_arr, width)
    a_re = stage_a[0, :, :, 0] + stage_a[1, :, :, 1]
    a_im = stage_a[0, :, :, 1] - stage_a[1, :, :, 0]
    mid_cos, mid_sin = angle_table(dev_ids, lane_blk, seg_len)
    mid_cos = mid_cos[:, None, None, :]
    mid_sin = mid_sin[:, None, None, :]
    b_re = (a_re * mid_cos + a_im * mid_sin).reshape(devices, pair, n_arr, block_w, channels)
    b_im = (a_im * mid_cos - a_re * mid_sin).reshape(devices, pair, n_arr, block_w, channels)
    m_cos, m_sin = angle_table(blk_ids, blk_ids, block_w)

    def blk_mix(table, vals):
        return jnp.einsum(
            "mb,qkzbc->qkzmc", table, vals, preferred_element_type=jnp.float32, precision=exact_mode
        )

    s_re = blk_mix(m_cos, b_re) + blk_mix(m_sin, b_im)
    s_im = blk_mix(m_cos, b_im) - blk_mix(m_sin, b_re)
    sig_r, cot_r, tap_r = (s_re[:, :, 0], s_re[:, :, 1], s_re[:, :, 2])
    sig_i, cot_i, tap_i = (s_im[:, :, 0], s_im[:, :, 1], s_im[:, :, 2])
    prod_r = jnp.stack(
        [
            sig_r * tap_r - sig_i * tap_i,
            cot_r * tap_r + cot_i * tap_i,
            cot_r * sig_r + cot_i * sig_i,
        ],
        axis=2,
    )
    prod_i = jnp.stack(
        [
            sig_r * tap_i + sig_i * tap_r,
            cot_i * tap_r - cot_r * tap_i,
            cot_i * sig_r - cot_r * sig_i,
        ],
        axis=2,
    )
    u_re = blk_mix(m_cos, prod_r) - blk_mix(m_sin, prod_i)
    u_im = blk_mix(m_cos, prod_i) + blk_mix(m_sin, prod_r)
    u_re = u_re.reshape(devices, pair, n_arr, width)
    u_im = u_im.reshape(devices, pair, n_arr, width)
    v_re = u_re * mid_cos - u_im * mid_sin
    v_im = u_im * mid_cos + u_re * mid_sin
    v_all = jnp.stack([v_re, v_im]).reshape(2 * devices, -1)
    inv_mat = jnp.concatenate(
        [jnp.concatenate([q_cos, -q_sin], axis=1), jnp.concatenate([q_sin, q_cos], axis=1)], axis=0
    )
    w_all = mat_dot(inv_mat, v_all).reshape(2, devices, pair, n_arr, width)
    b_rows = dev_ids[:, None] * block_w + lane_blk[None, :]
    k1_own = rank_seq * pair + jnp.arange(pair, dtype=jnp.int32)
    ex_ang = b_rows[:, None, :] * k1_own[None, :, None] % fft_size
    ex_ang = ex_ang.astype(jnp.float32) * (2.0 * math.pi / fft_size)
    ex_cos = jnp.cos(ex_ang)[:, :, None, :]
    ex_sin = jnp.sin(ex_ang)[:, :, None, :]
    x_re = w_all[0] * ex_cos - w_all[1] * ex_sin
    x_im = w_all[0] * ex_sin + w_all[1] * ex_cos
    back = jnp.stack([x_re, x_im], axis=1)
    back = lax.all_to_all(back, "seq", split_axis=0, concat_axis=0, tiled=True)
    back = back.reshape(devices, 2, pair, n_arr * width)
    back = jnp.transpose(back, (1, 0, 2, 3)).reshape(2 * rows_all, n_arr * width)
    out_mat = jnp.concatenate([col_cos.T, -col_sin.T], axis=1)
    res = (mat_dot(out_mat, back) * inv_scale).reshape(devices, n_arr, width)
    rows_out = lax.all_to_all(
        res[:, 0:2].astype(jnp.bfloat16), "seq", split_axis=0, concat_axis=0, tiled=True
    )
    conv_out = rows_out[:, 0].reshape(1, seg_len // 2, 2 * channels)
    d_signal = rows_out[:, 1].reshape(1, seg_len // 2, 2 * channels)
    d_taps = res[:, 2].reshape(devices * block_w, channels)
    d_raw = d_taps * envelope
    d_preact = mat_dot(d_raw, w_out.T) * jnp.cos(preact)
    out_part = mat_dot(hidden.T, d_raw)
    embed_part = mat_dot(features.T, d_preact)
    bias_part = jnp.sum(d_preact, axis=0)
    out_sum = lax.psum(out_part, "seq")
    embed_all, bias_all = lax.psum((embed_part, bias_part), ("seq", "chan"))
    norm_scale = 1.0 / math.sqrt(seq_total)
    return (conv_out, d_signal, embed_all * norm_scale, bias_all * norm_scale, out_sum * norm_scale)


def solution(mesh):
    return jax.shard_map(
        local,
        mesh=mesh,
        in_specs=(
            P("chan", "seq", None),
            P("chan", "seq", None),
            P(),
            P(),
            P(),
            P(None, "chan"),
            P("chan"),
        ),
        out_specs=(P("chan", "seq", None), P("chan", "seq", None), P(), P(), P(None, "chan")),
        check_vma=False,
    )
```

profile of v0, /device:TPU:0, one launch (start us, length us, event | category | flops | bytes accessed | tf_op | source)
XLA Modules:
  0.0 615.8 jit_solution(7838954913175535610)
XLA Ops:
  0.6 1.2 stack_reshape.8
  1.9 1.2 stack_reshape.9
  3.1 1.3 pad_maximum_fusion.14
  4.4 9.9 %all-to-all-start = ((bf16[64,2,1024]{2,1,0:T(2,128)(2,1)}), bf16[64,2,1024]{2,1,0:T(2,128)(2,1)S(1)}, u32[]{:S(2)}, u32[]{:S(2)}) async-start(bf16[64,2,1024]{2,1,0:T(2,128)(2,1)} %pad_maximum_fusion.14), calls=%async_computation | async-start | bytes 524288 | tf_op jit(solution)/shard_map/all_to_all | solution.py:60
  14.5 0.7 fusion.180
  15.2 1.0 fusion.84
  16.2 2.7 fusion.181
  19.9 2.0 fusion.35
  21.9 2.3 all-to-all-done
  24.9 1.9 convolution_negate_fusion
  26.8 2.3 add_bitcast_fusion.2
  29.3 4.1 copy.76
  33.4 6.9 %all-to-all-start.1 = ((f32[128,2,3,1024]{3,1,2,0:T(2,128)}), f32[128,2,3,1024]{3,1,2,0:T(2,128)S(1)}, u32[]{:S(2)}, u32[]{:S(2)}) async-start(f32[128,2,3,1024]{3,1,2,0:T(2,128)} %copy.76), calls=%async_computation.1 | async-start | bytes 6291456 | tf_op jit(solution)/shard_map/all_to_all | solution.py:77
  40.3 0.8 fusion.100
  42.6 1.8 fusion.44
  44.4 2.9 fusion.33
  47.2 9.5 %fusion.38 = (f32[64,2,1024]{2,1,0:T(2,128)}, f32[64,2,1024]{2,1,0:T(2,128)}) fusion(s32[2]{0:T(128)S(1)} %iota_add_fusion.1, s32[64,1024]{1,0:T(8,128)S(1)} %broadcast_add_fusion), kind=kLoop, calls=%fused_computation.88 | loop fusion | flops 1835008 | bytes 1310728 | tf_op jit(solution)/shard_map/cos | solution.py:130
  56.8 23.2 %all-to-all-done.1 = f32[128,2,3,1024]{3,1,2,0:T(2,128)S(1)} async-done(((f32[128,2,3,1024]{3,1,2,0:T(2,128)}), f32[128,2,3,1024]{3,1,2,0:T(2,128)S(1)}, u32[]{:S(2)}, u32[]{:S(2)}) %all-to-all-start.1) | async-done | bytes 3145760 | tf_op jit(solution)/shard_map/all_to_all | solution.py:77
  80.0 3.7 copy.77
  83.7 4.3 reshape.397
  88.0 3.7 dot_general.72
  91.8 9.4 %fusion = f32[2,64,2,2,3,1024]{5,1,4,3,2,0:T(8,128)S(1)} fusion(f32[2,64,64,1,1,1]{2,1,5,4,3,0:T(8,128)} %bitcast.98, f32[2,2,3,1024,64]{3,2,1,0,4:T(4,128)} %dot_general.72), kind=kOutput, calls=%fused_computation.6 | convolution fusion | flops 1207959552 | bytes 9469952 | tf_op jit(solution)/shard_map/dot_general | solution.py:11
  101.2 2.7 slice_add_fusion
  103.8 2.5 add.319
  106.4 3.6 sub.92
  110.0 5.5 fusion.51
  115.5 3.3 fusion.52
  118.8 3.3 add_bitcast_fusion.1
  122.1 3.5 subtract_bitcast_fusion.1
  126.2 0.7 multiply_subtract_fusion.5
  126.9 3.0 fusion.4
  130.0 2.9 fusion.3
  132.9 4.7 subtract_bitcast_fusion
  137.6 4.9 reshape.411
  142.5 6.4 %add_bitcast_fusion = f32[64,2,3,16,64]{4,3,2,1,0:T(8,128)} fusion(f32[64,2,3,64,16]{3,4,2,1,0:T(8,128)S(1)} %fusion.3, f32[64,2,1,16,64]{4,3,2,1,0:T(8,128)} %copy-done.5, f32[64,2,1,16,64]{4,3,2,1,0:T(8,128)} %copy-done.6, f32[64,2,1,16,64]{4,3,2,1,0:T(8,128)} %copy-done.4), kind=kOutput, calls=%fused_computation.9 | convolution fusion | flops 76680704 | bytes 4718592 | tf_op jit(solution)/shard_map/mb,qkzbc->qkzmc/dot_general | solution.py:91
  148.9 4.6 reshape.412
  153.6 3.3 multiply_subtract_fusion.2
  157.1 4.1 copy.85
  161.2 5.0 reshape.400
  166.2 3.8 fusion.63
  170.0 1.8 fusion.179
  171.9 3.1 squeeze.4
  174.9 3.9 squeeze.5
  178.9 2.4 multiply_subtract_fusion.1
  181.3 1.6 pad_maximum_fusion
  182.9 4.7 copy.86
  187.5 6.6 %all-to-all-start.2 = ((f32[64,2,2,3,1024]{4,2,3,1,0:T(2,128)}), f32[64,2,2,3,1024]{4,2,3,1,0:T(2,128)S(1)}, u32[]{:S(2)}, u32[]{:S(2)}) async-start(f32[64,2,2,3,1024]{4,2,3,1,0:T(2,128)} %copy.86), calls=%async_computation.2 | async-start | bytes 6291456 | tf_op jit(solution)/shard_map/all_to_all | solution.py:135
  194.1 0.8 sine_negate_fusion
  194.9 38.9 %all-to-all-done.2 = f32[64,2,2,3,1024]{4,2,3,1,0:T(2,128)S(1)} async-done(((f32[64,2,2,3,1024]{4,2,3,1,0:T(2,128)}), f32[64,2,2,3,1024]{4,2,3,1,0:T(2,128)S(1)}, u32[]{:S(2)}, u32[]{:S(2)}) %all-to-all-start.2) | async-done | bytes 3145760 | tf_op jit(solution)/shard_map/all_to_all | solution.py:135
  233.8 3.6 copy.87
  237.4 5.0 reshape.401
  242.3 4.1 copy.88
  246.4 3.9 reshape.402
  250.3 3.7 convolution_multiply_fusion
  254.0 1.7 reshape.403
  255.7 0.7 slice_reduce_fusion
  256.5 0.9 slice.117
  258.2 1.3 fusion.182
  259.9 64.6 %all-reduce = (f32[32,64]{1,0:T(8,128)S(1)}, f32[64]{0:T(128)S(1)}) all-reduce(f32[32,64]{1,0:T(8,128)S(1)} %fusion.53, f32[64]{0:T(128)S(1)} %get-tuple-element.41), channel_id=1, replica_groups=mesh['seq'=64,'chan'=2] {'seq','chan'}, use_global_device_ids=true, to_apply=%region_0.1 | all-reduce | flops 2112 | bytes 16896 | tf_op jit(solution)/shard_map/psum | solution.py:152
  325.1 5.9 all-to-all-start.3
  331.5 280.7 %psum.23 = f32[64,64]{1,0:T(8,128)S(1)} all-reduce(f32[64,64]{1,0:T(8,128)S(1)} %fusion.40), channel_id=1, replica_groups=mesh['seq'=64,'chan'=2] {'seq'}, use_global_device_ids=true, to_apply=%region_3.4 | all-reduce | flops 4096 | bytes 32768 | tf_op jit(solution)/shard_map/psum | solution.py:151
  612.8 1.1 slice_reduce_fusion.1
  613.9 0.7 reshape_squeeze.10
  614.6 0.7 reshape_squeeze.9
  (61 shorter events, 7.2 us)
Async XLA Ops:
  0.6 18.3 %copy-start = (f32[64,64]{1,0:T(8,128)S(1)}, f32[64,64]{1,0:T(8,128)}, u32[]{:S(2)}) copy-start(f32[64,64]{1,0:T(8,128)} %param.12) | copy-start | bytes 49156
  4.4 19.8 %all-to-all-start = ((bf16[64,2,1024]{2,1,0:T(2,128)(2,1)}), bf16[64,2,1024]{2,1,0:T(2,128)(2,1)S(1)}, u32[]{:S(2)}, u32[]{:S(2)}) async-start(bf16[64,2,1024]{2,1,0:T(2,128)(2,1)} %pad_maximum_fusion.14), calls=%async_computation | async-start | bytes 524288 | tf_op jit(solution)/shard_map/all_to_all | solution.py:60
  16.2 2.7 copy-start.13
  33.4 46.6 %all-to-all-start.1 = ((f32[128,2,3,1024]{3,1,2,0:T(2,128)}), f32[128,2,3,1024]{3,1,2,0:T(2,128)S(1)}, u32[]{:S(2)}, u32[]{:S(2)}) async-start(f32[128,2,3,1024]{3,1,2,0:T(2,128)} %copy.76), calls=%async_computation.1 | async-start | bytes 6291456 | tf_op jit(solution)/shard_map/all_to_all | solution.py:77
  41.2 0.6 copy-start.15
  109.9 5.5 copy-start.1
  110.0 5.5 copy-start.2
  110.0 5.5 copy-start.3
  126.2 6.8 %copy-start.6 = (f32[64,2,1,16,64]{4,3,2,1,0:T(8,128)}, f32[64,2,1,16,64]{4,3,2,1,0:T(8,128)S(1)}, u32[]{:S(2)}) copy-start(f32[64,2,1,16,64]{4,3,2,1,0:T(8,128)S(1)} %get-tuple-element.13) | copy-start | bytes 1572868
  126.9 6.0 copy-start.4
  126.9 6.0 copy-start.5
  148.9 4.6 copy-start.7
  148.9 4.6 copy-start.10
  148.9 4.6 copy-start.11
  171.9 7.0 %copy-start.8 = (f32[64,2,1024]{2,1,0:T(2,128)S(1)}, f32[64,2,1024]{2,1,0:T(2,128)}, u32[]{:S(2)}) copy-start(f32[64,2,1024]{2,1,0:T(2,128)} %get-tuple-element.25) | copy-start | bytes 1572868
  171.9 7.0 %copy-start.9 = (f32[64,2,1024]{2,1,0:T(2,128)S(1)}, f32[64,2,1024]{2,1,0:T(2,128)}, u32[]{:S(2)}) copy-start(f32[64,2,1024]{2,1,0:T(2,128)} %get-tuple-element.26) | copy-start | bytes 1572868
  187.5 46.3 %all-to-all-start.2 = ((f32[64,2,2,3,1024]{4,2,3,1,0:T(2,128)}), f32[64,2,2,3,1024]{4,2,3,1,0:T(2,128)S(1)}, u32[]{:S(2)}, u32[]{:S(2)}) async-start(f32[64,2,2,3,1024]{4,2,3,1,0:T(2,128)} %copy.86), calls=%async_computation.2 | async-start | bytes 6291456 | tf_op jit(solution)/shard_map/all_to_all | solution.py:135
  254.0 4.2 copy-start.12
  254.0 5.6 copy-start.14
  325.1 287.8 %all-to-all-start.3 = ((bf16[64,2,1024]{2,1,0:T(2,128)(2,1)}), bf16[64,2,1024]{2,1,0:T(2,128)(2,1)S(1)}, u32[]{:S(2)}, u32[]{:S(2)}) async-start(bf16[64,2,1024]{2,1,0:T(2,128)(2,1)} %slice.117), calls=%async_computation.3 | async-start | bytes 524288 | tf_op jit(solution)/shard_map/all_to_all | solution.py:140
where the time goes:
time: 627 us; the launch traced here: 616 us
  blocking collectives  345 us (55%)
  local copies, waits for them, and re-layouts  80.4 us (13%)
  waiting for transfers between devices  64.5 us (10%)
  matrix products  58.9 us (9%)
  other arithmetic  35.8 us (6%)
  starting transfers between devices  29.3 us (5%)
    psum x1, blocking collectives, local(): out_sum = lax.psum(out_part, 'seq')  281 us
    psum x1, blocking collectives, local(): embed_all, bias_all = lax.psum((embed_part, bias_part), ('seq', 'chan'))  64.6 us
    all_to_all x1, waiting for transfers between devices, local(): back = lax.all_to_all(back, 'seq', split_axis=0, concat_axis=0, tiled=True)  38.9 us
    dot_general x8, matrix products, blk_mix(): jnp.einsum('mb,qkzbc->qkzmc', table, vals, preferred_element_type=jnp.flo...  32.6 us
    dot_general x10, matrix products, mat_dot(): jnp.dot(lhs_mat, rhs_mat, preferred_element_type=jnp.float32, precision=e...  26.2 us
    all_to_all x1, waiting for transfers between devices, local(): spec = lax.all_to_all(spec, 'seq', split_axis=0, concat_axis=0, tiled=True)  23.2 us
  transfers between devices with their start and end apart: 4, of which 3 were waited for; matrix products, arithmetic and copies ran while one was open for 4% of the time, Pallas kernels for 0%

commit v1 on v0

--- a/solution.py
+++ b/solution.py
@@ -148,7 +148,8 @@
     out_part = mat_dot(hidden.T, d_raw)
     embed_part = mat_dot(features.T, d_preact)
     bias_part = jnp.sum(d_preact, axis=0)
-    out_sum = lax.psum(out_part, "seq")
+    parts = lax.all_gather(out_part, "seq")
+    out_sum = jnp.sum(parts, axis=0)
     embed_all, bias_all = lax.psum((embed_part, bias_part), ("seq", "chan"))
     norm_scale = 1.0 / math.sqrt(seq_total)
     return (conv_out, d_signal, embed_all * norm_scale, bias_all * norm_scale, out_sum * norm_scale)

time: 627 us -> 383 us (0.61)
  blocking collectives: 345 us -> 67.7 us
  waiting for transfers between devices: 64.5 us -> 87.6 us
  between operations: 1.63 us -> 14.8 us
    psum x1 -> x0, blocking collectives: 281 us -> none  [local(): out_sum = lax.psum(out_part, 'seq')]
    all_gather x0 -> x1, waiting for transfers between devices: none -> 23.1 us  [local(): parts = lax.all_gather(out_part, 'seq')]
  transfers between devices with their start and end apart: 4 -> 5, of which waited for: 3 -> 4; matrix products, arithmetic and copies ran while one was open for 4% -> 8% of each run, Pallas kernels for 0% -> 0%
where the time goes in v1:
time: 383 us; the launch traced here: 378 us
  waiting for transfers between devices  87.6 us (23%)
  local copies, waits for them, and re-layouts  80.6 us (21%)
  blocking collectives  67.7 us (18%)
  matrix products  59.5 us (16%)
  other arithmetic  37.6 us (10%)
  starting transfers between devices  29.9 us (8%)
  between operations  14.8 us (4%)
    psum x1, blocking collectives, local(): embed_all, bias_all = lax.psum((embed_part, bias_part), ('seq', 'chan'))  67.7 us
    all_to_all x1, waiting for transfers between devices, local(): back = lax.all_to_all(back, 'seq', split_axis=0, concat_axis=0, tiled=True)  38.9 us
    dot_general x8, matrix products, blk_mix(): jnp.einsum('mb,qkzbc->qkzmc', table, vals, preferred_element_type=jnp.flo...  32.7 us
    dot_general x10, matrix products, mat_dot(): jnp.dot(lhs_mat, rhs_mat, preferred_element_type=jnp.float32, precision=e...  26.8 us
    all_to_all x1, waiting for transfers between devices, local(): spec = lax.all_to_all(spec, 'seq', split_axis=0, concat_axis=0, tiled=True)  23.3 us
    all_gather x1, waiting for transfers between devices, local(): parts = lax.all_gather(out_part, 'seq')  23.1 us
    all_to_all x1, starting transfers between devices, local(): cols = lax.all_to_all(src, 'seq', split_axis=0, concat_axis=0, tiled=True)  10.1 us
    cos x1, other arithmetic, local(): ex_cos = jnp.cos(ex_ang)[:, :, None, :]  9.49 us
  transfers between devices with their start and end apart: 5, of which 4 were waited for; matrix products, arithmetic and copies ran while one was open for 8% of the time, Pallas kernels for 0%

profile of v1, /device:TPU:0, one launch (start us, length us, event | category | flops | bytes accessed | tf_op | source)
XLA Modules:
  0.0 377.8 jit_solution(7627434886997407737)
XLA Ops:
  7.2 1.2 stack_reshape.8
  8.4 1.2 stack_reshape.9
  9.7 1.3 pad_maximum_fusion.14
  11.0 10.1 %all-to-all-start = ((bf16[64,2,1024]{2,1,0:T(2,128)(2,1)}), bf16[64,2,1024]{2,1,0:T(2,128)(2,1)S(1)}, u32[]{:S(2)}, u32[]{:S(2)}) async-start(bf16[64,2,1024]{2,1,0:T(2,128)(2,1)} %pad_maximum_fusion.14), calls=%async_computation | async-start | bytes 524288 | tf_op jit(solution)/shard_map/all_to_all | solution.py:60
  21.9 1.0 fusion.84
  22.9 2.6 fusion.181
  26.6 2.0 fusion.35
  28.6 2.3 all-to-all-done
  31.6 1.9 convolution_negate_fusion
  33.5 2.3 add_bitcast_fusion.2
  36.0 4.1 %copy.76 = f32[128,2,3,1024]{3,1,2,0:T(2,128)} copy(f32[128,2,3,1024]{3,0,2,1:T(8,128)S(1)} %pad_maximum_fusion.1) | data formatting | bytes 6291456 | tf_op jit(solution)/shard_map/stack | solution.py:76
  40.1 7.0 %all-to-all-start.1 = ((f32[128,2,3,1024]{3,1,2,0:T(2,128)}), f32[128,2,3,1024]{3,1,2,0:T(2,128)S(1)}, u32[]{:S(2)}, u32[]{:S(2)}) async-start(f32[128,2,3,1024]{3,1,2,0:T(2,128)} %copy.76), calls=%async_computation.1 | async-start | bytes 6291456 | tf_op jit(solution)/shard_map/all_to_all | solution.py:77
  47.2 0.7 fusion.100
  49.4 1.8 fusion.44
  51.2 2.9 fusion.33
  54.1 9.5 %fusion.38 = (f32[64,2,1024]{2,1,0:T(2,128)}, f32[64,2,1024]{2,1,0:T(2,128)}) fusion(s32[2]{0:T(128)S(1)} %iota_add_fusion.1, s32[64,1024]{1,0:T(8,128)S(1)} %broadcast_add_fusion), kind=kLoop, calls=%fused_computation.88 | loop fusion | flops 1835008 | bytes 1310728 | tf_op jit(solution)/shard_map/cos | solution.py:130
  63.6 23.3 %all-to-all-done.1 = f32[128,2,3,1024]{3,1,2,0:T(2,128)S(1)} async-done(((f32[128,2,3,1024]{3,1,2,0:T(2,128)}), f32[128,2,3,1024]{3,1,2,0:T(2,128)S(1)}, u32[]{:S(2)}, u32[]{:S(2)}) %all-to-all-start.1) | async-done | bytes 3145760 | tf_op jit(solution)/shard_map/all_to_all | solution.py:77
  86.9 3.7 copy.77
  90.6 4.3 %reshape.397 = f32[64,12288]{1,0:T(8,128)S(1)} reshape(f32[128,2,3,1024]{3,2,1,0:T(4,128)} %copy.77) | data formatting | bytes 6291456 | tf_op jit(solution)/shard_map/reshape | solution.py:79
  94.9 3.7 dot_general.72
  98.6 9.4 %fusion = f32[2,64,2,2,3,1024]{5,1,4,3,2,0:T(8,128)S(1)} fusion(f32[2,64,64,1,1,1]{2,1,5,4,3,0:T(8,128)} %bitcast.100, f32[2,2,3,1024,64]{3,2,1,0,4:T(4,128)} %dot_general.72), kind=kOutput, calls=%fused_computation.6 | convolution fusion | flops 1207959552 | bytes 9469952 | tf_op jit(solution)/shard_map/dot_general | solution.py:11
  108.0 2.7 slice_add_fusion
  110.7 2.5 add.317
  113.2 3.6 sub.92
  116.8 5.5 %fusion.51 = f32[64,2,3,64,16]{3,4,2,1,0:T(8,128)S(1)} fusion(f32[64,2,3,16,64]{4,3,0,2,1:T(8,128)} %sub.92, f32[64,2,3,16,64]{4,3,0,2,1:T(8,128)S(1)} %add.317, f32[64,16,64]{2,1,0:T(8,128)} %get-tuple-element.30, f32[64,16,64]{2,1,0:T(8,128)} %get-tuple-element.29), kind=kOutput, calls=%fused_computation.104 | convolution fusion | flops 76680704 | bytes 5242880 | tf_op jit(solution)/shard_map/mb,qkzbc->qkzmc/dot_general | solution.py:91
  122.4 3.3 fusion.52
  125.7 3.3 add_bitcast_fusion.1
  129.0 3.5 subtract_bitcast_fusion.1
  133.0 0.7 multiply_subtract_fusion.5
  133.8 3.0 fusion.4
  136.8 2.9 fusion.3
  139.8 4.7 %subtract_bitcast_fusion = f32[64,2,3,16,64]{4,3,2,1,0:T(8,128)} fusion(f32[64,2,3,64,16]{3,4,2,1,0:T(8,128)S(1)} %fusion.4, f32[64,2,1,16,64]{4,3,2,1,0:T(8,128)S(1)} %get-tuple-element.10, f32[64,2,1,16,64]{4,3,2,1,0:T(8,128)S(1)} %get-tuple-element.13, f32[64,2,1,16,64]{4,3,2,1,0:T(8,128)S(1)} %get-tuple-element.9), kind=kOutput, calls=%fused_computation.10 | convolution fusion | flops 76680704 | bytes 4718592 | tf_op jit(solution)/shard_map/mb,qkzbc->qkzmc/dot_general | solution.py:91
  144.5 4.9 %reshape.412 = f32[1,64,2,3,1024]{4,3,2,1,0:T(4,128)} reshape(f32[64,2,3,16,64]{4,3,2,1,0:T(8,128)} %subtract_bitcast_fusion) | data formatting | bytes 3145728 | tf_op jit(solution)/shard_map/reshape | solution.py:117
  149.4 6.4 %add_bitcast_fusion = f32[64,2,3,16,64]{4,3,2,1,0:T(8,128)} fusion(f32[64,2,3,64,16]{3,4,2,1,0:T(8,128)S(1)} %fusion.3, f32[64,2,1,16,64]{4,3,2,1,0:T(8,128)} %copy-done.5, f32[64,2,1,16,64]{4,3,2,1,0:T(8,128)} %copy-done.6, f32[64,2,1,16,64]{4,3,2,1,0:T(8,128)} %copy-done.4), kind=kOutput, calls=%fused_computation.9 | convolution fusion | flops 76680704 | bytes 4718592 | tf_op jit(solution)/shard_map/mb,qkzbc->qkzmc/dot_general | solution.py:91
  155.8 4.6 %reshape.413 = f32[1,64,2,3,1024]{4,3,2,1,0:T(4,128)} reshape(f32[64,2,3,16,64]{4,3,2,1,0:T(8,128)} %add_bitcast_fusion) | data formatting | bytes 3145728 | tf_op jit(solution)/shard_map/reshape | solution.py:118
  160.5 3.3 multiply_subtract_fusion.2
  164.0 4.1 %copy.85 = f32[2,64,2,3,1024]{4,3,2,1,0:T(4,128)} copy(f32[2,64,2,3,1024]{4,1,3,2,0:T(8,128)S(1)} %pad_maximum_fusion.4) | data formatting | bytes 6291456 | tf_op jit(solution)/shard_map/stack | solution.py:121
  168.1 5.0 %reshape.400 = f32[128,6144]{1,0:T(8,128)S(1)} reshape(f32[2,64,2,3,1024]{4,3,2,1,0:T(4,128)} %copy.85) | data formatting | bytes 6291456 | tf_op jit(solution)/shard_map/reshape | solution.py:121
  173.1 3.8 %fusion.63 = f32[128,6144]{1,0:T(8,128)S(1)} fusion(f32[128,6144]{1,0:T(8,128)S(1)} %reshape.400, f32[64,64]{1,0:T(8,128)} %copy-done.15, f32[64,64]{1,0:T(8,128)S(1)} %get-tuple-element.43, f32[64,64]{1,0:T(8,128)} %fusion.100), kind=kOutput, calls=%fused_computation.121 | convolution fusion | flops 1208008704 | bytes 6340608 | tf_op jit(solution)/shard_map/dot_general | solution.py:11
  176.9 1.8 fusion.179
  178.8 3.1 squeeze.4
  181.8 3.9 %squeeze.5 = f32[64,1,2,3,1024]{4,3,2,0,1:T(4,128)} reshape(f32[64,6144]{1,0:T(8,128)} %get-tuple-element.24) | data formatting | bytes 3145728 | tf_op jit(solution)/shard_map/squeeze | solution.py:132
  185.8 2.4 multiply_subtract_fusion.1
  188.2 1.6 pad_maximum_fusion
  189.8 4.7 %copy.86 = f32[64,2,2,3,1024]{4,2,3,1,0:T(2,128)} copy(f32[64,2,2,3,1024]{4,3,2,0,1:T(4,128)S(1)} %pad_maximum_fusion) | data formatting | bytes 6291456 | tf_op jit(solution)/shard_map/stack | solution.py:134
  194.4 6.4 %all-to-all-start.2 = ((f32[64,2,2,3,1024]{4,2,3,1,0:T(2,128)}), f32[64,2,2,3,1024]{4,2,3,1,0:T(2,128)S(1)}, u32[]{:S(2)}, u32[]{:S(2)}) async-start(f32[64,2,2,3,1024]{4,2,3,1,0:T(2,128)} %copy.86), calls=%async_computation.2 | async-start | bytes 6291456 | tf_op jit(solution)/shard_map/all_to_all | solution.py:135
  200.9 0.8 sine_negate_fusion
  201.6 38.9 %all-to-all-done.2 = f32[64,2,2,3,1024]{4,2,3,1,0:T(2,128)S(1)} async-done(((f32[64,2,2,3,1024]{4,2,3,1,0:T(2,128)}), f32[64,2,2,3,1024]{4,2,3,1,0:T(2,128)S(1)}, u32[]{:S(2)}, u32[]{:S(2)}) %all-to-all-start.2) | async-done | bytes 3145760 | tf_op jit(solution)/shard_map/all_to_all | solution.py:135
  240.6 3.6 copy.87
  244.2 5.2 %reshape.401 = f32[64,2,2,3072]{3,0,2,1:T(8,128)S(1)} reshape(f32[64,2,2,3,1024]{4,3,0,2,1:T(4,128)} %copy.87) | data formatting | bytes 6291456 | tf_op jit(solution)/shard_map/reshape | solution.py:136
  249.3 4.1 %copy.88 = f32[2,64,2,3072]{3,2,1,0:T(2,128)} copy(f32[2,64,2,3072]{3,1,2,0:T(8,128)S(1)} %bitcast.96) | data formatting | bytes 6291456 | tf_op jit(solution)/shard_map/transpose | solution.py:137
  253.4 3.9 %reshape.402 = f32[256,3072]{1,0:T(8,128)S(1)} reshape(f32[2,64,2,3072]{3,2,1,0:T(2,128)} %copy.88) | data formatting | bytes 6291456 | tf_op jit(solution)/shard_map/reshape | solution.py:137
  257.3 3.7 convolution_multiply_fusion
  260.9 1.7 reshape.403
  262.7 0.7 slice_reduce_fusion
  263.8 1.1 fusion.40
  264.9 0.9 slice.117
  265.8 6.4 %all-to-all-start.3 = ((bf16[64,2,1024]{2,1,0:T(2,128)(2,1)}), bf16[64,2,1024]{2,1,0:T(2,128)(2,1)S(1)}, u32[]{:S(2)}, u32[]{:S(2)}) async-start(bf16[64,2,1024]{2,1,0:T(2,128)(2,1)} %slice.117), calls=%async_computation.3 | async-start | bytes 524288 | tf_op jit(solution)/shard_map/all_to_all | solution.py:140
  272.2 1.4 fusion.182
  273.9 67.7 %all-reduce = (f32[32,64]{1,0:T(8,128)S(1)}, f32[64]{0:T(128)S(1)}) all-reduce(f32[32,64]{1,0:T(8,128)S(1)} %fusion.53, f32[64]{0:T(128)S(1)} %get-tuple-element.41), channel_id=1, replica_groups=mesh['seq'=64,'chan'=2] {'seq','chan'}, use_global_device_ids=true, to_apply=%region_0.1 | all-reduce | flops 2112 | bytes 16896 | tf_op jit(solution)/shard_map/psum | solution.py:153
  342.7 1.1 slice_reduce_fusion.1
  343.8 0.7 reshape_squeeze.10
  345.2 23.1 %all-gather.3.cloned.1.call-done = f32[4096,64]{1,0:T(8,128)} async-done(((f32[64,64]{1,0:T(8,128)}), f32[4096,64]{1,0:T(8,128)}) %all-gather.3.cloned.1.call-update) | async-done | bytes 1048592 | tf_op jit(solution)/shard_map/all_gather | solution.py:151
  368.3 1.8 reduce_sum.19
  (64 shorter events, 8.1 us)
Async XLA Ops:
  7.2 18.4 %copy-start = (f32[64,64]{1,0:T(8,128)S(1)}, f32[64,64]{1,0:T(8,128)}, u32[]{:S(2)}) copy-start(f32[64,64]{1,0:T(8,128)} %param.12) | copy-start | bytes 49156
  11.0 20.0 %all-to-all-start = ((bf16[64,2,1024]{2,1,0:T(2,128)(2,1)}), bf16[64,2,1024]{2,1,0:T(2,128)(2,1)S(1)}, u32[]{:S(2)}, u32[]{:S(2)}) async-start(bf16[64,2,1024]{2,1,0:T(2,128)(2,1)} %pad_maximum_fusion.14), calls=%async_computation | async-start | bytes 524288 | tf_op jit(solution)/shard_map/all_to_all | solution.py:60
  22.9 2.7 copy-start.13
  40.1 46.8 %all-to-all-start.1 = ((f32[128,2,3,1024]{3,1,2,0:T(2,128)}), f32[128,2,3,1024]{3,1,2,0:T(2,128)S(1)}, u32[]{:S(2)}, u32[]{:S(2)}) async-start(f32[128,2,3,1024]{3,1,2,0:T(2,128)} %copy.76), calls=%async_computation.1 | async-start | bytes 6291456 | tf_op jit(solution)/shard_map/all_to_all | solution.py:77
  48.1 0.6 copy-start.15
  116.8 5.5 %copy-start.1 = (f32[64,2,3,16,64]{4,3,0,2,1:T(8,128)S(1)}, f32[64,2,3,16,64]{4,3,0,2,1:T(8,128)}, u32[]{:S(2)}) copy-start(f32[64,2,3,16,64]{4,3,0,2,1:T(8,128)} %sub.92) | copy-start | bytes 4718596
  116.8 5.5 %copy-start.2 = (f32[64,16,64]{2,1,0:T(8,128)S(1)}, f32[64,16,64]{2,1,0:T(8,128)}, u32[]{:S(2)}) copy-start(f32[64,16,64]{2,1,0:T(8,128)} %get-tuple-element.29) | copy-start | bytes 786436
  116.8 5.5 %copy-start.3 = (f32[64,16,64]{2,1,0:T(8,128)S(1)}, f32[64,16,64]{2,1,0:T(8,128)}, u32[]{:S(2)}) copy-start(f32[64,16,64]{2,1,0:T(8,128)} %get-tuple-element.30) | copy-start | bytes 786436
  133.0 6.8 %copy-start.6 = (f32[64,2,1,16,64]{4,3,2,1,0:T(8,128)}, f32[64,2,1,16,64]{4,3,2,1,0:T(8,128)S(1)}, u32[]{:S(2)}) copy-start(f32[64,2,1,16,64]{4,3,2,1,0:T(8,128)S(1)} %get-tuple-element.13) | copy-start | bytes 1572868
  133.8 6.0 %copy-start.4 = (f32[64,2,1,16,64]{4,3,2,1,0:T(8,128)}, f32[64,2,1,16,64]{4,3,2,1,0:T(8,128)S(1)}, u32[]{:S(2)}) copy-start(f32[64,2,1,16,64]{4,3,2,1,0:T(8,128)S(1)} %get-tuple-element.9) | copy-start | bytes 1572868
  133.8 6.0 %copy-start.5 = (f32[64,2,1,16,64]{4,3,2,1,0:T(8,128)}, f32[64,2,1,16,64]{4,3,2,1,0:T(8,128)S(1)}, u32[]{:S(2)}) copy-start(f32[64,2,1,16,64]{4,3,2,1,0:T(8,128)S(1)} %get-tuple-element.10) | copy-start | bytes 1572868
  155.8 4.6 %copy-start.7 = (f32[1,64,2,3,1024]{4,3,2,1,0:T(4,128)S(1)}, f32[1,64,2,3,1024]{4,3,2,1,0:T(4,128)}, u32[]{:S(2)}) copy-start(f32[1,64,2,3,1024]{4,3,2,1,0:T(4,128)} %reshape.412) | copy-start | bytes 4718596
  155.8 4.6 %copy-start.10 = (f32[64,1024]{1,0:T(8,128)S(1)}, f32[64,1024]{1,0:T(8,128)}, u32[]{:S(2)}) copy-start(f32[64,1024]{1,0:T(8,128)} %get-tuple-element.31) | copy-start | bytes 786436
  155.8 4.6 %copy-start.11 = (f32[64,1024]{1,0:T(8,128)S(1)}, f32[64,1024]{1,0:T(8,128)}, u32[]{:S(2)}) copy-start(f32[64,1024]{1,0:T(8,128)} %get-tuple-element.32) | copy-start | bytes 786436
  178.8 7.0 %copy-start.8 = (f32[64,2,1024]{2,1,0:T(2,128)S(1)}, f32[64,2,1024]{2,1,0:T(2,128)}, u32[]{:S(2)}) copy-start(f32[64,2,1024]{2,1,0:T(2,128)} %get-tuple-element.25) | copy-start | bytes 1572868
  178.8 7.0 %copy-start.9 = (f32[64,2,1024]{2,1,0:T(2,128)S(1)}, f32[64,2,1024]{2,1,0:T(2,128)}, u32[]{:S(2)}) copy-start(f32[64,2,1024]{2,1,0:T(2,128)} %get-tuple-element.26) | copy-start | bytes 1572868
  194.4 46.2 %all-to-all-start.2 = ((f32[64,2,2,3,1024]{4,2,3,1,0:T(2,128)}), f32[64,2,2,3,1024]{4,2,3,1,0:T(2,128)S(1)}, u32[]{:S(2)}, u32[]{:S(2)}) async-start(f32[64,2,2,3,1024]{4,2,3,1,0:T(2,128)} %copy.86), calls=%async_computation.2 | async-start | bytes 6291456 | tf_op jit(solution)/shard_map/all_to_all | solution.py:135
  200.8 167.5 %all-gather.3.cloned.1.call-start = ((), (), s32[]{:S(2)}) async-start(), calls=%async_computation.4 | async-start | bytes 2129920 | tf_op jit(solution)/shard_map/all_gather | solution.py:151
  260.9 11.3 %copy-start.12 = (f32[1024,64]{0,1:T(8,128)S(1)}, f32[1024,64]{0,1:T(8,128)}, u32[]{:S(2)}) copy-start(f32[1024,64]{0,1:T(8,128)} %get-tuple-element.40) | copy-start | bytes 786436
  260.9 12.6 %copy-start.14 = (f32[1024,16]{0,1:T(8,128)S(1)}, f32[1024,16]{0,1:T(8,128)}, u32[]{:S(2)}) copy-start(f32[1024,16]{0,1:T(8,128)} %copy-done.13) | copy-start | bytes 196612
  265.8 76.9 %all-to-all-start.3 = ((bf16[64,2,1024]{2,1,0:T(2,128)(2,1)}), bf16[64,2,1024]{2,1,0:T(2,128)(2,1)S(1)}, u32[]{:S(2)}, u32[]{:S(2)}) async-start(bf16[64,2,1024]{2,1,0:T(2,128)(2,1)} %slice.117), calls=%async_computation.3 | async-start | bytes 524288 | tf_op jit(solution)/shard_map/all_to_all | solution.py:140
Sparse Core Ops, SparseCore 0:
  265.0 103.2 all-gather.2
